TPU v7x, 32 devices: a whole 2x2x4 slice. The times are simulated.
32 devices in a mesh: dp: 4 (over z), expert: 8 (over y, x, core).
Axes of the slice: x: 2, y: 2, z: 4, core: 2. Of those that a mesh axis runs over, the one named last changes fastest.
Arguments:
- tokens: bfloat16 [384, 4096], P('expert', 'dp'), may hold values from -6 to 6
- out_grad: bfloat16 [384, 4096], P('expert', 'dp'), may hold values from -6 to 6
- expert_ids: int32 [384, 8], P('expert'), may hold values from 0 to 63, all different within a row; in each aligned block of 48 rows (0 to 47, 48 to 95, ...) at most 12 rows name the same one
- route_weights: float32 [384, 8], P('expert'), may hold values from 0.05 to 1
- gate_weight: bfloat16 [64, 4096, 768], P('expert', 'dp'), may hold values from -0.09375 to 0.09375
- up_weight: bfloat16 [64, 4096, 768], P('expert', 'dp'), may hold values from -0.09375 to 0.09375
- down_weight: bfloat16 [64, 768, 4096], P('expert', None, 'dp'), may hold values from -0.21875 to 0.21875
Outputs:
- layer_out: bfloat16 [384, 4096], P('expert', 'dp')
- grad_tokens: bfloat16 [384, 4096], P('expert', 'dp')
- gate_grad: bfloat16 [64, 4096, 768], P('expert', 'dp')
- up_grad: bfloat16 [64, 4096, 768], P('expert', 'dp')
- down_grad: bfloat16 [64, 768, 4096], P('expert', None, 'dp')
Inputs may be any that keep to these rules, and one draw needn't show every extreme that they name: `expert_ids`: each row names 8 different experts. In the 48 rows of one index of the expert axis no expert is named more than 12 times, and in every draw some expert is named exactly 12 times there.
All inputs are finite; a program needn't handle non-finite values.
Results may differ from a plain program's by a relative error of at most 0.029.
Values may be sent and summed in bfloat16 or wider, within the bound.
No kernel may reach another device: no remote copies, remote signals or barrier semaphores. Data moves between devices by JAX's collectives and lax.ppermute only.
A program may use at most 128 MiB of HBM per device.

v0:
```python
import jax
import jax.numpy as jnp
from jax import lax
from jax.sharding import PartitionSpec as P


def swiglu_parts(gate_sum, up_sum, back_sum):
    logistic = jax.nn.sigmoid(gate_sum)
    activated = gate_sum * logistic
    hidden = (activated * up_sum).astype(jnp.bfloat16)
    gate_delta = (back_sum * up_sum * logistic * (1.0 + gate_sum * (1.0 - logistic))).astype(
        jnp.bfloat16
    )
    up_delta = (back_sum * activated).astype(jnp.bfloat16)
    return (hidden, gate_delta, up_delta)


def split_f32(value):
    high = value.astype(jnp.bfloat16)
    rest = value - high.astype(jnp.float32)
    middle = rest.astype(jnp.bfloat16)
    low = (rest - middle.astype(jnp.float32)).astype(jnp.bfloat16)
    return (high, middle, low)


def local(tokens, out_grad, expert_ids, route_weights, gate_weight, up_weight, down_weight):
    token_count, width_dev = tokens.shape
    per_token = expert_ids.shape[1]
    local_experts = gate_weight.shape[0]
    hidden_units = gate_weight.shape[2]
    sources = lax.axis_size("expert")
    experts = local_experts * sources
    capacity = 2 * token_count * per_token // experts
    slot_count = token_count * per_token
    me = lax.axis_index("expert")
    high, middle, low = split_f32(route_weights)
    route_cols = 4 * per_token
    pad_cols = -route_cols % 128
    packed = jnp.concatenate(
        [
            tokens,
            out_grad,
            expert_ids.astype(jnp.bfloat16),
            high,
            middle,
            low,
            jnp.zeros((token_count, pad_cols), jnp.bfloat16),
        ],
        axis=1,
    )
    gathered = lax.all_to_all(
        jnp.broadcast_to(packed[None], (sources,) + packed.shape).reshape(
            sources * token_count, packed.shape[1]
        ),
        "expert",
        split_axis=0,
        concat_axis=0,
        tiled=True,
    )
    feats = gathered[:, : 2 * width_dev]
    route_all = gathered[:, 2 * width_dev : 2 * width_dev + route_cols].astype(jnp.float32)
    ids_all = route_all[:, :per_token].astype(jnp.int32)
    w_all = (
        route_all[:, per_token : 2 * per_token]
        + route_all[:, 2 * per_token : 3 * per_token]
        + route_all[:, 3 * per_token :]
    )
    all_tokens = sources * token_count
    flat_all = ids_all.reshape(sources, slot_count)
    position = jnp.arange(slot_count, dtype=jnp.int32)
    earlier = (flat_all[:, None, :] == flat_all[:, :, None]) & (
        position[None, None, :] < position[None, :, None]
    )
    rank_all = jnp.sum(earlier.astype(jnp.int32), axis=2)
    local_e = flat_all - me * local_experts
    is_local = (local_e >= 0) & (local_e < local_experts)
    src = jnp.arange(sources, dtype=jnp.int32)[:, None]
    row_count = local_experts * sources * capacity
    row_of = jnp.where(is_local, (local_e * sources + src) * capacity + rank_all, row_count)
    row_of = row_of.reshape(sources * slot_count)
    token_of = jnp.arange(sources * slot_count, dtype=jnp.int32) // per_token
    target = jnp.arange(row_count, dtype=jnp.int32)
    hit = target[:, None] == row_of[None, :]
    holder = jnp.sum(jnp.where(hit, token_of[None, :] + 1, 0), axis=1) - 1
    row_weight = jnp.sum(jnp.where(hit, w_all.reshape(-1)[None, :], 0.0), axis=1)
    select = (holder[:, None] == jnp.arange(all_tokens, dtype=jnp.int32)[None, :]).astype(
        jnp.bfloat16
    )
    picked = jnp.dot(select, feats, preferred_element_type=jnp.float32)
    x_in = picked[:, :width_dev].astype(jnp.bfloat16)
    dy_in = (row_weight[:, None] * picked[:, width_dev:]).astype(jnp.bfloat16)
    x_in = x_in.reshape(local_experts, sources * capacity, width_dev)
    dy_in = dy_in.reshape(local_experts, sources * capacity, width_dev)
    gate_part = jnp.einsum(
        "jrd,jdf->jrf", x_in, gate_weight, preferred_element_type=jnp.float32
    ).astype(jnp.bfloat16)
    up_part = jnp.einsum(
        "jrd,jdf->jrf", x_in, up_weight, preferred_element_type=jnp.float32
    ).astype(jnp.bfloat16)
    front = jnp.concatenate([gate_part, up_part], axis=2).reshape(row_count, 2 * hidden_units)
    front_sums = lax.psum_scatter(front, "dp", scatter_dimension=0, tiled=True)
    back_part = jnp.einsum(
        "jrd,jfd->jrf", dy_in, down_weight, preferred_element_type=jnp.float32
    ).astype(jnp.bfloat16)
    dp_count = lax.axis_size("dp")
    back_blocks = lax.all_to_all(
        back_part.reshape(row_count, hidden_units), "dp", split_axis=0, concat_axis=0, tiled=True
    )
    back_sums = jnp.sum(
        back_blocks.reshape(dp_count, row_count // dp_count, hidden_units).astype(jnp.float32),
        axis=0,
    )
    front_sums = front_sums.astype(jnp.float32)
    hidden, gate_delta, up_delta = swiglu_parts(
        front_sums[:, :hidden_units], front_sums[:, hidden_units:], back_sums
    )
    hidden = lax.all_gather(hidden, "dp", axis=0, tiled=True)
    deltas = lax.all_gather(
        jnp.concatenate([gate_delta, up_delta], axis=1), "dp", axis=0, tiled=True
    )
    expert_shape = (local_experts, sources, capacity, hidden_units)
    hidden = hidden.reshape(expert_shape)
    gate_delta = deltas[:, :hidden_units].reshape(expert_shape)
    up_delta = deltas[:, hidden_units:].reshape(expert_shape)
    rows_shape = (local_experts, sources * capacity, hidden_units)
    buffer_rows = experts * capacity
    expert_out = jnp.einsum(
        "jrf,jfd->jrd", hidden.reshape(rows_shape), down_weight, preferred_element_type=jnp.float32
    ).astype(jnp.bfloat16)
    expert_out = expert_out.reshape(local_experts, sources, capacity, width_dev).transpose(
        1, 0, 2, 3
    )
    out_back = lax.all_to_all(
        expert_out.reshape(buffer_rows, width_dev),
        "expert",
        split_axis=0,
        concat_axis=0,
        tiled=True,
    )
    down_grad = jnp.einsum(
        "jrf,jrd->jfd", hidden.reshape(rows_shape), dy_in, preferred_element_type=jnp.float32
    ).astype(jnp.bfloat16)
    expert_back = (
        jnp.einsum(
            "jrf,jdf->jrd",
            gate_delta.reshape(rows_shape),
            gate_weight,
            preferred_element_type=jnp.float32,
        )
        + jnp.einsum(
            "jrf,jdf->jrd",
            up_delta.reshape(rows_shape),
            up_weight,
            preferred_element_type=jnp.float32,
        )
    ).astype(jnp.bfloat16)
    expert_back = expert_back.reshape(local_experts, sources, capacity, width_dev).transpose(
        1, 0, 2, 3
    )
    grad_back = lax.all_to_all(
        expert_back.reshape(buffer_rows, width_dev),
        "expert",
        split_axis=0,
        concat_axis=0,
        tiled=True,
    )
    gate_grad = jnp.einsum(
        "jrd,jrf->jdf", x_in, gate_delta.reshape(rows_shape), preferred_element_type=jnp.float32
    ).astype(jnp.bfloat16)
    up_grad = jnp.einsum(
        "jrd,jrf->jdf", x_in, up_delta.reshape(rows_shape), preferred_element_type=jnp.float32
    ).astype(jnp.bfloat16)
    flat_ids = expert_ids.reshape(slot_count)
    earlier_local = (flat_ids[None, :] == flat_ids[:, None]) & (
        position[None, :] < position[:, None]
    )
    slot_rank = jnp.sum(earlier_local.astype(jnp.int32), axis=1)
    slot_place = (flat_ids * capacity + slot_rank).reshape(token_count, per_token)
    picked_out = jnp.take(out_back, slot_place, axis=0).astype(jnp.float32)
    layer_out = jnp.sum(picked_out * route_weights[:, :, None], axis=1).astype(jnp.bfloat16)
    picked_back = jnp.take(grad_back, slot_place, axis=0).astype(jnp.float32)
    grad_tokens = jnp.sum(picked_back, axis=1).astype(jnp.bfloat16)
    return (layer_out, grad_tokens, gate_grad, up_grad, down_grad)


def solution(mesh):
    in_specs = (
        P("expert", "dp"),
        P("expert", "dp"),
        P("expert", None),
        P("expert", None),
        P("expert", "dp", None),
        P("expert", "dp", None),
        P("expert", None, "dp"),
    )
    out_specs = (
        P("expert", "dp"),
        P("expert", "dp"),
        P("expert", "dp", None),
        P("expert", "dp", None),
        P("expert", None, "dp"),
    )
    return jax.shard_map(local, mesh=mesh, in_specs=in_specs, out_specs=out_specs, check_vma=False)
```

profile of v0, /device:TPU:0, one launch (start us, length us, event | category | flops | bytes accessed | tf_op | source)
XLA Modules:
  0.0 272.1 jit_solution(667128261609481006)
XLA Ops:
  11.3 5.2 %all-to-all-start = ((bf16[8,48,2176]{2,1,0:T(8,128)(2,1)}), bf16[8,48,2176]{2,1,0:T(8,128)(2,1)S(1)}, u32[]{:S(2)}, u32[]{:S(2)}) async-start(bf16[8,48,2176]{2,1,0:T(8,128)(2,1)} %broadcast_in_dim.60), calls=%async_computation | async-start | bytes 3342336 | tf_op jit(solution)/shard_map/all_to_all | solution.py:51
  16.6 22.0 %all-to-all-done = bf16[8,48,2176]{2,1,0:T(8,128)(2,1)S(1)} async-done(((bf16[8,48,2176]{2,1,0:T(8,128)(2,1)}), bf16[8,48,2176]{2,1,0:T(8,128)(2,1)S(1)}, u32[]{:S(2)}, u32[]{:S(2)}) %all-to-all-start) | async-done | bytes 1671200 | tf_op jit(solution)/shard_map/all_to_all | solution.py:51
  44.1 3.2 %copy-done.1 = f32[768,2048]{1,0:T(8,128)} copy-done((f32[768,2048]{1,0:T(8,128)}, f32[768,2048]{1,0:T(8,128)S(1)}, u32[]{:S(2)}) %copy-start.1) | copy-done | bytes 6291480
  49.1 2.0 convolution_convert_fusion.5
  51.1 6.6 %convolution_convert_fusion.6 = bf16[8,96,768]{2,1,0:T(8,128)(2,1)S(1)} fusion(bf16[8,96,1024]{2,1,0:T(8,128)(2,1)S(1)} %bitcast.45, bf16[8,1024,768]{2,1,0:T(8,128)(2,1)} %param.13), kind=kOutput, calls=%fused_computation.21 | convolution fusion | flops 1208549376 | bytes 15335424 | tf_op jit(solution)/shard_map/jrd,jdf->jrf/dot_general | solution.py:94
  60.9 2.1 fusion
  63.0 9.6 %convolution_convert_fusion.4 = bf16[8,96,768]{2,1,0:T(8,128)(2,1)S(1)} fusion(bf16[8,96,1024]{2,1,0:T(8,128)(2,1)S(1)} %bitcast.50, bf16[8,768,1024]{2,1,0:T(8,128)(2,1)} %param.15), kind=kOutput, calls=%fused_computation.19 | convolution fusion | flops 1208549376 | bytes 15335424 | tf_op jit(solution)/shard_map/jrd,jfd->jrf/dot_general | solution.py:102
  72.6 58.2 %all_to_all.42 = bf16[4,192,768]{2,1,0:T(8,128)(2,1)S(1)} all-to-all(bf16[4,192,768]{2,1,0:T(8,128)(2,1)S(1)} %bitcast.63), channel_id=1, replica_groups=mesh['dp'=4,'expert'=8] {'dp'}, dimensions={0} | all-to-all | bytes 2359296 | tf_op jit(solution)/shard_map/all_to_all | solution.py:106
  134.2 28.9 %all-gather.3.cloned.1.call-done = bf16[768,768]{1,0:T(8,128)(2,1)} async-done(((bf16[192,768]{1,0:T(8,128)(2,1)}), bf16[768,768]{1,0:T(8,128)(2,1)}) %all-gather.3.cloned.1.call-update) | async-done | bytes 1179664 | tf_op jit(solution)/shard_map/all_gather | solution.py:117
  163.1 7.1 %convolution_convert_fusion.3 = bf16[8,96,1024]{2,1,0:T(8,128)(2,1)S(1)} fusion(bf16[8,96,768]{2,1,0:T(8,128)(2,1)} %bitcast.64, bf16[8,768,1024]{2,1,0:T(8,128)(2,1)} %param.15), kind=kOutput, calls=%fused_computation.15 | convolution fusion | flops 1208745984 | bytes 15335424 | tf_op jit(solution)/shard_map/jrf,jfd->jrd/dot_general | solution.py:127
  173.9 3.9 %all-to-all-start.1 = ((bf16[8,96,1024]{2,1,0:T(8,128)(2,1)}), bf16[8,96,1024]{2,1,0:T(8,128)(2,1)S(1)}, u32[]{:S(2)}, u32[]{:S(2)}) async-start(bf16[8,96,1024]{2,1,0:T(8,128)(2,1)} %copy.70), calls=%async_computation.2 | async-start | bytes 3145728 | tf_op jit(solution)/shard_map/all_to_all | solution.py:133
  178.9 10.0 %convolution_convert_fusion = bf16[8,768,1024]{2,1,0:T(8,128)(2,1)} fusion(bf16[8,96,768]{2,1,0:T(8,128)(2,1)} %bitcast.65, bf16[8,96,1024]{2,1,0:T(8,128)(2,1)} %bitcast.51), kind=kOutput, calls=%fused_computation.5 | convolution fusion | flops 1214251008 | bytes 15335424 | tf_op jit(solution)/shard_map/jrf,jrd->jfd/dot_general | solution.py:140
  188.9 9.9 %all-to-all-done.1 = bf16[8,96,1024]{2,1,0:T(8,128)(2,1)S(1)} async-done(((bf16[8,96,1024]{2,1,0:T(8,128)(2,1)}), bf16[8,96,1024]{2,1,0:T(8,128)(2,1)S(1)}, u32[]{:S(2)}, u32[]{:S(2)}) %all-to-all-start.1) | async-done | bytes 1572896 | tf_op jit(solution)/shard_map/all_to_all | solution.py:133
  198.8 2.7 gather_fusion
  201.4 12.9 %all-gather.5.cloned.1.call-done = bf16[768,1536]{1,0:T(8,128)(2,1)} async-done(((bf16[192,1536]{1,0:T(8,128)(2,1)}), bf16[768,1536]{1,0:T(8,128)(2,1)}) %all-gather.5.cloned.1.call-update) | async-done | bytes 2359312 | tf_op jit(solution)/shard_map/all_gather | solution.py:118
  216.1 9.3 %fusion.12 = f32[8,96,1024]{2,1,0:T(8,128)S(1)} fusion(bf16[8,96,768]{2,1,0:T(8,128)(2,1)S(1)} %bitcast.52, bf16[8,1024,768]{2,1,0:T(8,128)(2,1)} %param.13), kind=kOutput, calls=%fused_computation.58 | convolution fusion | flops 1207959552 | bytes 16908288 | tf_op jit(solution)/shard_map/jrf,jdf->jrd/dot_general | solution.py:144
  225.5 8.5 %add_convert_fusion = bf16[8,96,1024]{2,1,0:T(8,128)(2,1)S(1)} fusion(f32[8,96,1024]{2,1,0:T(8,128)S(1)} %fusion.12, bf16[8,96,768]{2,1,0:T(8,128)(2,1)S(1)} %bitcast.54, bf16[8,1024,768]{2,1,0:T(8,128)(2,1)} %param.14), kind=kOutput, calls=%fused_computation.12 | convolution fusion | flops 1209532416 | bytes 18481152 | tf_op jit(solution)/shard_map/jrf,jdf->jrd/dot_general | solution.py:150
  235.7 2.0 copy.76
  237.7 3.8 %all-to-all-start.3 = ((bf16[8,96,1024]{2,1,0:T(8,128)(2,1)}), bf16[8,96,1024]{2,1,0:T(8,128)(2,1)S(1)}, u32[]{:S(2)}, u32[]{:S(2)}) async-start(bf16[8,96,1024]{2,1,0:T(8,128)(2,1)} %copy.76), calls=%async_computation.4 | async-start | bytes 3145728 | tf_op jit(solution)/shard_map/all_to_all | solution.py:160
  241.6 2.4 multiply_reduce_fusion
  244.0 8.0 %convolution_convert_fusion.1 = bf16[8,1024,768]{2,1,0:T(8,128)(2,1)} fusion(bf16[8,96,1024]{2,1,0:T(8,128)(2,1)S(1)} %bitcast.46, bf16[8,96,768]{2,1,0:T(8,128)(2,1)} %bitcast.55), kind=kOutput, calls=%fused_computation.6 | convolution fusion | flops 1214251008 | bytes 15335424 | tf_op jit(solution)/shard_map/jrd,jrf->jdf/dot_general | solution.py:170
  252.0 6.6 %convolution_convert_fusion.2 = bf16[8,1024,768]{2,1,0:T(8,128)(2,1)} fusion(bf16[8,96,1024]{2,1,0:T(8,128)(2,1)S(1)} %bitcast.47, bf16[8,96,768]{2,1,0:T(8,128)(2,1)S(1)} %bitcast.53), kind=kOutput, calls=%fused_computation.7 | convolution fusion | flops 1214251008 | bytes 15335424 | tf_op jit(solution)/shard_map/jrd,jrf->jdf/dot_general | solution.py:167
  258.6 3.8 %all-to-all-done.3 = bf16[8,96,1024]{2,1,0:T(8,128)(2,1)S(1)} async-done(((bf16[8,96,1024]{2,1,0:T(8,128)(2,1)}), bf16[8,96,1024]{2,1,0:T(8,128)(2,1)S(1)}, u32[]{:S(2)}, u32[]{:S(2)}) %all-to-all-start.3) | async-done | bytes 1572896 | tf_op jit(solution)/shard_map/all_to_all | solution.py:160
  262.4 2.1 gather_fusion.1
  (73 shorter events, 27.3 us)
Async XLA Ops:
  11.3 27.3 %all-to-all-start = ((bf16[8,48,2176]{2,1,0:T(8,128)(2,1)}), bf16[8,48,2176]{2,1,0:T(8,128)(2,1)S(1)}, u32[]{:S(2)}, u32[]{:S(2)}) async-start(bf16[8,48,2176]{2,1,0:T(8,128)(2,1)} %broadcast_in_dim.60), calls=%async_computation | async-start | bytes 3342336 | tf_op jit(solution)/shard_map/all_to_all | solution.py:51
  16.5 114.5 %reduce-scatter.2.cloned.1.call-start = ((), (), s32[]{:S(2)}) async-start(), calls=%async_computation.5 | async-start | bytes 2949120 | tf_op jit(solution)/shard_map/reduce_scatter | solution.py:101
  42.2 6.9 %copy-start = (bf16[8,1024,768]{2,1,0:T(8,128)(2,1)S(1)}, bf16[8,1024,768]{2,1,0:T(8,128)(2,1)}, u32[]{:S(2)}) copy-start(bf16[8,1024,768]{2,1,0:T(8,128)(2,1)} %param.14) | copy-start | bytes 37748740
  44.1 3.2 %copy-start.1 = (f32[768,2048]{1,0:T(8,128)}, f32[768,2048]{1,0:T(8,128)S(1)}, u32[]{:S(2)}) copy-start(f32[768,2048]{1,0:T(8,128)S(1)} %fusion.1) | copy-start | bytes 18874372
  59.3 103.8 %all-gather.3.cloned.1.call-start = ((), (), s32[]{:S(2)}) async-start(), calls=%async_computation.6 | async-start | bytes 1474560 | tf_op jit(solution)/shard_map/all_gather | solution.py:117
  63.0 9.6 %copy-start.2 = (bf16[768,1024]{1,0:T(8,128)(2,1)}, bf16[768,1024]{1,0:T(8,128)(2,1)S(1)}, u32[]{:S(2)}) copy-start(bf16[768,1024]{1,0:T(8,128)(2,1)S(1)} %fusion) | copy-start | bytes 4718596
  133.3 81.0 %all-gather.5.cloned.1.call-start = ((), (), s32[]{:S(2)}) async-start(), calls=%async_computation.7 | async-start | bytes 2949120 | tf_op jit(solution)/shard_map/all_gather | solution.py:118
  173.9 3.9 %copy-start.7 = (f32[48,8]{0,1:T(8,128)S(1)}, f32[48,8]{0,1:T(8,128)}, u32[]{:S(2)}) copy-start(f32[48,8]{0,1:T(8,128)} %param.12) | copy-start | bytes 4612
  173.9 4.0 %copy-start.6 = (s32[48,8]{0,1:T(8,128)S(1)}, s32[48,8]{0,1:T(8,128)}, u32[]{:S(2)}) copy-start(s32[48,8]{0,1:T(8,128)} %param.11) | copy-start | bytes 4612
  173.9 24.8 %all-to-all-start.1 = ((bf16[8,96,1024]{2,1,0:T(8,128)(2,1)}), bf16[8,96,1024]{2,1,0:T(8,128)(2,1)S(1)}, u32[]{:S(2)}, u32[]{:S(2)}) async-start(bf16[8,96,1024]{2,1,0:T(8,128)(2,1)} %copy.70), calls=%async_computation.2 | async-start | bytes 3145728 | tf_op jit(solution)/shard_map/all_to_all | solution.py:133
  216.1 9.3 %copy-start.3 = (bf16[768,768]{1,0:T(8,128)(2,1)}, bf16[768,768]{1,0:T(8,128)(2,1)S(1)}, u32[]{:S(2)}) copy-start(bf16[768,768]{1,0:T(8,128)(2,1)S(1)} %get-tuple-element.9) | copy-start | bytes 3538948
  216.1 9.3 %copy-start.5 = (bf16[768,768]{1,0:T(8,128)(2,1)}, bf16[768,768]{1,0:T(8,128)(2,1)S(1)}, u32[]{:S(2)}) copy-start(bf16[768,768]{1,0:T(8,128)(2,1)S(1)} %get-tuple-element.8) | copy-start | bytes 3538948
  237.7 24.7 %all-to-all-start.3 = ((bf16[8,96,1024]{2,1,0:T(8,128)(2,1)}), bf16[8,96,1024]{2,1,0:T(8,128)(2,1)S(1)}, u32[]{:S(2)}, u32[]{:S(2)}) async-start(bf16[8,96,1024]{2,1,0:T(8,128)(2,1)} %copy.76), calls=%async_computation.4 | async-start | bytes 3145728 | tf_op jit(solution)/shard_map/all_to_all | solution.py:160
  244.0 8.0 %copy-start.4 = (bf16[768,768]{1,0:T(8,128)(2,1)S(1)}, bf16[768,768]{1,0:T(8,128)(2,1)}, u32[]{:S(2)}) copy-start(bf16[768,768]{1,0:T(8,128)(2,1)} %copy-done.3) | copy-start | bytes 3538948
Sparse Core Ops, SparseCore 0:
  59.4 66.0 reduce-scatter.1
  133.4 29.6 all-gather.2
  164.7 49.5 all-gather.4
where the time goes:
time: 273 us; the launch traced here: 272 us
  waiting for transfers between devices  77.5 us (28%)
  matrix products  69.5 us (25%)
  blocking collectives  58.2 us (21%)
  local copies, waits for them, and re-layouts  23 us (8%)
  other arithmetic  16.6 us (6%)
  between operations  14.1 us (5%)
  starting transfers between devices  13.2 us (5%)
    all_to_all x1, blocking collectives, local(): lax.all_to_all(back_part.reshape(row_count, hidden_units), 'dp', split_ax...  58.2 us
    all_gather x1, waiting for transfers between devices, local(): hidden = lax.all_gather(hidden, 'dp', axis=0, tiled=True)  28.9 us
    all_to_all x1, waiting for transfers between devices, local(): lax.all_to_all(jnp.broadcast_to(packed[None], (sources,) + packed.shape)....  22 us
    all_gather x1, waiting for transfers between devices, local(): lax.all_gather(jnp.concatenate([gate_delta, up_delta], axis=1), 'dp', axi...  12.9 us
    dot_general x1, matrix products, local(): jnp.einsum('jrf,jrd->jfd', hidden.reshape(rows_shape), dy_in, preferred_e...  10 us
    all_to_all x1, waiting for transfers between devices, local(): lax.all_to_all(expert_out.reshape(buffer_rows, width_dev), 'expert', spli...  9.89 us
    dot_general x1, matrix products, local(): jnp.einsum('jrd,jfd->jrf', dy_in, down_weight, preferred_element_type=jnp...  9.56 us
    dot_general x1, matrix products, local(): jnp.einsum('jrf,jdf->jrd', gate_delta.reshape(rows_shape), gate_weight, p...  9.3 us
  transfers between devices with their start and end apart: 6, of which 5 were waited for; matrix products, arithmetic and copies ran while one was open for 20% of the time, Pallas kernels for 0%

commit v1 on v0

--- a/solution.py
+++ b/solution.py
@@ -2,6 +2,24 @@
 import jax.numpy as jnp
 from jax import lax
 from jax.sharding import PartitionSpec as P
+
+
+def in_order(blocks, dim):
+    lengths = list(blocks.shape[1:])
+    lengths[dim] *= blocks.shape[0]
+    return jnp.moveaxis(blocks, 0, dim).reshape(lengths)
+
+
+def doubled(x, axis):
+    size = lax.axis_size(axis)
+    blocks = x[None]
+    for level in range(size.bit_length() - 1):
+        bit = 1 << level
+        received = lax.ppermute(blocks, axis, [(i, i ^ bit) for i in range(size)])
+        both = jnp.stack([blocks, received])
+        upper = lax.axis_index(axis) >> level & 1
+        blocks = jnp.where(upper == 0, both, both[::-1]).reshape(-1, *x.shape)
+    return blocks
 
 
 def swiglu_parts(gate_sum, up_sum, back_sum):
@@ -114,7 +132,7 @@
     hidden, gate_delta, up_delta = swiglu_parts(
         front_sums[:, :hidden_units], front_sums[:, hidden_units:], back_sums
     )
-    hidden = lax.all_gather(hidden, "dp", axis=0, tiled=True)
+    hidden = in_order(doubled(hidden, "dp"), 0)
     deltas = lax.all_gather(
         jnp.concatenate([gate_delta, up_delta], axis=1), "dp", axis=0, tiled=True
     )

time: 273 us -> 298 us (1.092)
  waiting for transfers between devices: 77.5 us -> 97.9 us
  starting transfers between devices: 13.2 us -> 17.4 us
    ppermute x0 -> x2, waiting for transfers between devices: none -> 62.1 us  [doubled(): received = lax.ppermute(blocks, axis, [(i, i ^ bit) for i in range(size)])]
    all_gather x1 -> x0, waiting for transfers between devices: 28.9 us -> none  [local(): hidden = lax.all_gather(hidden, 'dp', axis=0, tiled=True)]
    all_gather x1, waiting for transfers between devices: 12.9 us -> 0.01 us  [local(): lax.all_gather(jnp.concatenate([gate_delta, up_delta], axis=1), 'dp', axi...]
    ppermute x0 -> x2, starting transfers between devices: none -> 3.47 us  [doubled(): received = lax.ppermute(blocks, axis, [(i, i ^ bit) for i in range(size)])]
  transfers between devices with their start and end apart: 6 -> 7, of which waited for: 5 -> 5; matrix products, arithmetic and copies ran while one was open for 20% -> 19% of each run, Pallas kernels for 0% -> 0%
where the time goes in v1:
time: 298 us; the launch traced here: 297 us
  waiting for transfers between devices  97.9 us (33%)
  matrix products  69.6 us (23%)
  blocking collectives  58.2 us (20%)
  local copies, waits for them, and re-layouts  23 us (8%)
  starting transfers between devices  17.4 us (6%)
  other arithmetic  16.4 us (6%)
  between operations  14.4 us (5%)
    ppermute x2, waiting for transfers between devices, doubled(): received = lax.ppermute(blocks, axis, [(i, i ^ bit) for i in range(size)])  62.1 us
    all_to_all x1, blocking collectives, local(): lax.all_to_all(back_part.reshape(row_count, hidden_units), 'dp', split_ax...  58.2 us
    all_to_all x1, waiting for transfers between devices, local(): lax.all_to_all(jnp.broadcast_to(packed[None], (sources,) + packed.shape)....  22 us
    all_to_all x1, waiting for transfers between devices, local(): lax.all_to_all(expert_out.reshape(buffer_rows, width_dev), 'expert', spli...  10.1 us
    dot_general x1, matrix products, local(): jnp.einsum('jrf,jrd->jfd', hidden.reshape(rows_shape), dy_in, preferred_e...  10 us
    dot_general x1, matrix products, local(): jnp.einsum('jrd,jfd->jrf', dy_in, down_weight, preferred_element_type=jnp...  9.56 us
    dot_general x1, matrix products, local(): jnp.einsum('jrf,jdf->jrd', gate_delta.reshape(rows_shape), gate_weight, p...  9.31 us
    dot_general x1, matrix products, local(): jnp.einsum('jrf,jdf->jrd', up_delta.reshape(rows_shape), up_weight, prefe...  8.47 us
  transfers between devices with their start and end apart: 7, of which 5 were waited for; matrix products, arithmetic and copies ran while one was open for 19% of the time, Pallas kernels for 0%

profile of v1, /device:TPU:0, one launch (start us, length us, event | category | flops | bytes accessed | tf_op | source)
XLA Modules:
  0.0 296.9 jit_solution(2263988803650777588)
XLA Ops:
  11.3 5.2 %all-to-all-start = ((bf16[8,48,2176]{2,1,0:T(8,128)(2,1)}), bf16[8,48,2176]{2,1,0:T(8,128)(2,1)S(1)}, u32[]{:S(2)}, u32[]{:S(2)}) async-start(bf16[8,48,2176]{2,1,0:T(8,128)(2,1)} %broadcast_in_dim.63), calls=%async_computation | async-start | bytes 3342336 | tf_op jit(solution)/shard_map/all_to_all | solution.py:69
  16.6 22.0 %all-to-all-done = bf16[8,48,2176]{2,1,0:T(8,128)(2,1)S(1)} async-done(((bf16[8,48,2176]{2,1,0:T(8,128)(2,1)}), bf16[8,48,2176]{2,1,0:T(8,128)(2,1)S(1)}, u32[]{:S(2)}, u32[]{:S(2)}) %all-to-all-start) | async-done | bytes 1671200 | tf_op jit(solution)/shard_map/all_to_all | solution.py:69
  44.1 3.2 %copy-done.1 = f32[768,2048]{1,0:T(8,128)} copy-done((f32[768,2048]{1,0:T(8,128)}, f32[768,2048]{1,0:T(8,128)S(1)}, u32[]{:S(2)}) %copy-start.1) | copy-done | bytes 6291480
  49.1 2.0 convolution_convert_fusion.5
  51.1 6.6 %convolution_convert_fusion.6 = bf16[8,96,768]{2,1,0:T(8,128)(2,1)S(1)} fusion(bf16[8,96,1024]{2,1,0:T(8,128)(2,1)S(1)} %bitcast.53, bf16[8,1024,768]{2,1,0:T(8,128)(2,1)} %param.13), kind=kOutput, calls=%fused_computation.22 | convolution fusion | flops 1208549376 | bytes 15335424 | tf_op jit(solution)/shard_map/jrd,jdf->jrf/dot_general | solution.py:112
  60.9 2.1 fusion
  63.0 9.6 %convolution_convert_fusion.4 = bf16[8,96,768]{2,1,0:T(8,128)(2,1)S(1)} fusion(bf16[8,96,1024]{2,1,0:T(8,128)(2,1)S(1)} %bitcast.58, bf16[8,768,1024]{2,1,0:T(8,128)(2,1)} %param.15), kind=kOutput, calls=%fused_computation.20 | convolution fusion | flops 1208549376 | bytes 15335424 | tf_op jit(solution)/shard_map/jrd,jfd->jrf/dot_general | solution.py:120
  72.6 58.2 %all_to_all.42 = bf16[4,192,768]{2,1,0:T(8,128)(2,1)S(1)} all-to-all(bf16[4,192,768]{2,1,0:T(8,128)(2,1)S(1)} %bitcast.73), channel_id=1, replica_groups=mesh['dp'=4,'expert'=8] {'dp'}, dimensions={0} | all-to-all | bytes 2359296 | tf_op jit(solution)/shard_map/all_to_all | solution.py:124
  135.1 6.1 %collective-permute-done = bf16[1,192,768]{2,1,0:T(8,128)(2,1)S(1)} collective-permute-done((bf16[1,192,768]{2,1,0:T(8,128)(2,1)S(1)}, bf16[1,192,768]{2,1,0:T(8,128)(2,1)S(1)}, u32[]{:S(2)}, u32[]{:S(2)}) %collective-permute-start) | collective-permute-done | bytes 294944 | tf_op jit(solution)/shard_map/ppermute | solution.py:18
  143.2 56.0 %collective-permute-done.1 = bf16[2,192,768]{2,1,0:T(8,128)(2,1)S(1)} collective-permute-done((bf16[2,192,768]{2,1,0:T(8,128)(2,1)S(1)}, bf16[2,192,768]{2,1,0:T(8,128)(2,1)S(1)}, u32[]{:S(2)}, u32[]{:S(2)}) %collective-permute-start.1) | collective-permute-done | bytes 589856 | tf_op jit(solution)/shard_map/ppermute | solution.py:18
  199.6 7.2 %convolution_convert_fusion.3 = bf16[8,96,1024]{2,1,0:T(8,128)(2,1)S(1)} fusion(bf16[8,96,768]{2,1,0:T(8,128)(2,1)S(1)} %bitcast.64, bf16[8,768,1024]{2,1,0:T(8,128)(2,1)} %param.15), kind=kOutput, calls=%fused_computation.16 | convolution fusion | flops 1208745984 | bytes 15335424 | tf_op jit(solution)/shard_map/jrf,jfd->jrd/dot_general | solution.py:145
  210.6 4.6 %all-to-all-start.1 = ((bf16[8,96,1024]{2,1,0:T(8,128)(2,1)}), bf16[8,96,1024]{2,1,0:T(8,128)(2,1)S(1)}, u32[]{:S(2)}, u32[]{:S(2)}) async-start(bf16[8,96,1024]{2,1,0:T(8,128)(2,1)} %copy.70), calls=%async_computation.2 | async-start | bytes 3145728 | tf_op jit(solution)/shard_map/all_to_all | solution.py:151
  216.2 10.0 %convolution_convert_fusion = bf16[8,768,1024]{2,1,0:T(8,128)(2,1)} fusion(bf16[8,96,768]{2,1,0:T(8,128)(2,1)} %bitcast.65, bf16[8,96,1024]{2,1,0:T(8,128)(2,1)} %bitcast.59), kind=kOutput, calls=%fused_computation.5 | convolution fusion | flops 1214251008 | bytes 15335424 | tf_op jit(solution)/shard_map/jrf,jrd->jfd/dot_general | solution.py:158
  226.2 10.1 %all-to-all-done.1 = bf16[8,96,1024]{2,1,0:T(8,128)(2,1)S(1)} async-done(((bf16[8,96,1024]{2,1,0:T(8,128)(2,1)}), bf16[8,96,1024]{2,1,0:T(8,128)(2,1)S(1)}, u32[]{:S(2)}, u32[]{:S(2)}) %all-to-all-start.1) | async-done | bytes 1572896 | tf_op jit(solution)/shard_map/all_to_all | solution.py:151
  236.3 2.7 gather_fusion
  240.8 9.3 %fusion.14 = f32[8,96,1024]{2,1,0:T(8,128)S(1)} fusion(bf16[8,96,768]{2,1,0:T(8,128)(2,1)S(1)} %bitcast.60, bf16[8,1024,768]{2,1,0:T(8,128)(2,1)} %param.13), kind=kOutput, calls=%fused_computation.64 | convolution fusion | flops 1207959552 | bytes 16908288 | tf_op jit(solution)/shard_map/jrf,jdf->jrd/dot_general | solution.py:162
  250.1 8.5 %add_convert_fusion = bf16[8,96,1024]{2,1,0:T(8,128)(2,1)S(1)} fusion(f32[8,96,1024]{2,1,0:T(8,128)S(1)} %fusion.14, bf16[8,96,768]{2,1,0:T(8,128)(2,1)S(1)} %bitcast.62, bf16[8,1024,768]{2,1,0:T(8,128)(2,1)} %param.14), kind=kOutput, calls=%fused_computation.12 | convolution fusion | flops 1209532416 | bytes 18481152 | tf_op jit(solution)/shard_map/jrf,jdf->jrd/dot_general | solution.py:168
  260.3 2.0 copy.76
  262.3 3.8 %all-to-all-start.3 = ((bf16[8,96,1024]{2,1,0:T(8,128)(2,1)}), bf16[8,96,1024]{2,1,0:T(8,128)(2,1)S(1)}, u32[]{:S(2)}, u32[]{:S(2)}) async-start(bf16[8,96,1024]{2,1,0:T(8,128)(2,1)} %copy.76), calls=%async_computation.4 | async-start | bytes 3145728 | tf_op jit(solution)/shard_map/all_to_all | solution.py:178
  266.2 2.4 multiply_reduce_fusion
  268.6 8.0 %convolution_convert_fusion.1 = bf16[8,1024,768]{2,1,0:T(8,128)(2,1)} fusion(bf16[8,96,1024]{2,1,0:T(8,128)(2,1)S(1)} %bitcast.54, bf16[8,96,768]{2,1,0:T(8,128)(2,1)} %bitcast.63), kind=kOutput, calls=%fused_computation.6 | convolution fusion | flops 1214251008 | bytes 15335424 | tf_op jit(solution)/shard_map/jrd,jrf->jdf/dot_general | solution.py:188
  276.6 6.6 %convolution_convert_fusion.2 = bf16[8,1024,768]{2,1,0:T(8,128)(2,1)} fusion(bf16[8,96,1024]{2,1,0:T(8,128)(2,1)S(1)} %bitcast.55, bf16[8,96,768]{2,1,0:T(8,128)(2,1)S(1)} %bitcast.61), kind=kOutput, calls=%fused_computation.7 | convolution fusion | flops 1214251008 | bytes 15335424 | tf_op jit(solution)/shard_map/jrd,jrf->jdf/dot_general | solution.py:185
  283.2 3.7 %all-to-all-done.3 = bf16[8,96,1024]{2,1,0:T(8,128)(2,1)S(1)} async-done(((bf16[8,96,1024]{2,1,0:T(8,128)(2,1)}), bf16[8,96,1024]{2,1,0:T(8,128)(2,1)S(1)}, u32[]{:S(2)}, u32[]{:S(2)}) %all-to-all-start.3) | async-done | bytes 1572896 | tf_op jit(solution)/shard_map/all_to_all | solution.py:178
  286.9 2.1 gather_fusion.1
  (80 shorter events, 30.5 us)
Async XLA Ops:
  11.3 27.3 %all-to-all-start = ((bf16[8,48,2176]{2,1,0:T(8,128)(2,1)}), bf16[8,48,2176]{2,1,0:T(8,128)(2,1)S(1)}, u32[]{:S(2)}, u32[]{:S(2)}) async-start(bf16[8,48,2176]{2,1,0:T(8,128)(2,1)} %broadcast_in_dim.63), calls=%async_computation | async-start | bytes 3342336 | tf_op jit(solution)/shard_map/all_to_all | solution.py:69
  16.5 114.5 %reduce-scatter.2.cloned.1.call-start = ((), (), s32[]{:S(2)}) async-start(), calls=%async_computation.5 | async-start | bytes 2949120 | tf_op jit(solution)/shard_map/reduce_scatter | solution.py:119
  42.2 6.9 %copy-start = (bf16[8,1024,768]{2,1,0:T(8,128)(2,1)S(1)}, bf16[8,1024,768]{2,1,0:T(8,128)(2,1)}, u32[]{:S(2)}) copy-start(bf16[8,1024,768]{2,1,0:T(8,128)(2,1)} %param.14) | copy-start | bytes 37748740
  44.1 3.2 %copy-start.1 = (f32[768,2048]{1,0:T(8,128)}, f32[768,2048]{1,0:T(8,128)S(1)}, u32[]{:S(2)}) copy-start(f32[768,2048]{1,0:T(8,128)S(1)} %fusion.1) | copy-start | bytes 18874372
  59.3 179.7 %all-gather.2.cloned.1.call-start = ((), (), s32[]{:S(2)}) async-start(), calls=%async_computation.6 | async-start | bytes 2949120 | tf_op jit(solution)/shard_map/all_gather | solution.py:136
  63.0 9.6 %copy-start.2 = (bf16[768,1024]{1,0:T(8,128)(2,1)}, bf16[768,1024]{1,0:T(8,128)(2,1)S(1)}, u32[]{:S(2)}) copy-start(bf16[768,1024]{1,0:T(8,128)(2,1)S(1)} %fusion) | copy-start | bytes 4718596
  132.6 8.7 %collective-permute-start = (bf16[1,192,768]{2,1,0:T(8,128)(2,1)S(1)}, bf16[1,192,768]{2,1,0:T(8,128)(2,1)S(1)}, u32[]{:S(2)}, u32[]{:S(2)}) collective-permute-start(bf16[1,192,768]{2,1,0:T(8,128)(2,1)S(1)} %bitcast.74), channel_id=1, source_target_pairs={{0,8},{8,0},{16,24},{24,16},{1,9},{9,1},{17,25},{25,17},{2,10},{10... | collective-permute-start | bytes 884744 | tf_op jit(solution)/shard_map/ppermute | solution.py:18
  141.4 57.8 %collective-permute-start.1 = (bf16[2,192,768]{2,1,0:T(8,128)(2,1)S(1)}, bf16[2,192,768]{2,1,0:T(8,128)(2,1)S(1)}, u32[]{:S(2)}, u32[]{:S(2)}) collective-permute-start(bf16[2,192,768]{2,1,0:T(8,128)(2,1)S(1)} %get-tuple-element.14), channel_id=1, source_target_pairs={{0,16},{8,24},{16,0},{24,8},{1,17},{9,25},{17,1},{25,9},{2,18},{10... | collective-permute-start | bytes 1769480 | tf_op jit(solution)/shard_map/ppermute | solution.py:18
  199.6 7.3 %copy-start.6 = (bf16[2,2,192,768]{3,2,1,0:T(8,128)(2,1)}, bf16[2,2,192,768]{3,2,1,0:T(8,128)(2,1)S(1)}, u32[]{:S(2)}) copy-start(bf16[2,2,192,768]{3,2,1,0:T(8,128)(2,1)S(1)} %reverse_select_fusion) | copy-start | bytes 3538948
  210.6 4.7 %copy-start.8 = (f32[48,8]{0,1:T(8,128)S(1)}, f32[48,8]{0,1:T(8,128)}, u32[]{:S(2)}) copy-start(f32[48,8]{0,1:T(8,128)} %param.12) | copy-start | bytes 4612
  210.6 4.7 %copy-start.7 = (s32[48,8]{0,1:T(8,128)S(1)}, s32[48,8]{0,1:T(8,128)}, u32[]{:S(2)}) copy-start(s32[48,8]{0,1:T(8,128)} %param.11) | copy-start | bytes 4612
  210.6 25.7 %all-to-all-start.1 = ((bf16[8,96,1024]{2,1,0:T(8,128)(2,1)}), bf16[8,96,1024]{2,1,0:T(8,128)(2,1)S(1)}, u32[]{:S(2)}, u32[]{:S(2)}) async-start(bf16[8,96,1024]{2,1,0:T(8,128)(2,1)} %copy.70), calls=%async_computation.2 | async-start | bytes 3145728 | tf_op jit(solution)/shard_map/all_to_all | solution.py:151
  240.7 9.3 %copy-start.3 = (bf16[768,768]{1,0:T(8,128)(2,1)}, bf16[768,768]{1,0:T(8,128)(2,1)S(1)}, u32[]{:S(2)}) copy-start(bf16[768,768]{1,0:T(8,128)(2,1)S(1)} %get-tuple-element.9) | copy-start | bytes 3538948
  240.8 9.3 %copy-start.5 = (bf16[768,768]{1,0:T(8,128)(2,1)}, bf16[768,768]{1,0:T(8,128)(2,1)S(1)}, u32[]{:S(2)}) copy-start(bf16[768,768]{1,0:T(8,128)(2,1)S(1)} %get-tuple-element.8) | copy-start | bytes 3538948
  262.3 24.5 %all-to-all-start.3 = ((bf16[8,96,1024]{2,1,0:T(8,128)(2,1)}), bf16[8,96,1024]{2,1,0:T(8,128)(2,1)S(1)}, u32[]{:S(2)}, u32[]{:S(2)}) async-start(bf16[8,96,1024]{2,1,0:T(8,128)(2,1)} %copy.76), calls=%async_computation.4 | async-start | bytes 3145728 | tf_op jit(solution)/shard_map/all_to_all | solution.py:178
  268.6 8.0 %copy-start.4 = (bf16[768,768]{1,0:T(8,128)(2,1)S(1)}, bf16[768,768]{1,0:T(8,128)(2,1)}, u32[]{:S(2)}) copy-start(bf16[768,768]{1,0:T(8,128)(2,1)} %copy-done.3) | copy-start | bytes 3538948
Sparse Core Ops, SparseCore 0:
  59.4 66.0 reduce-scatter.1
  135.3 72.2 all-gather.1
